TPU v7x, 256 devices: a whole 4x4x8 slice. The times are simulated.
256 devices in a mesh: expert: 8 (over x, core), tensor: 32 (over z, y).
Axes of the slice: x: 4, y: 4, z: 8, core: 2. Of those that a mesh axis runs over, the one named last changes fastest.
Arguments:
- resid: bfloat16 [16384, 2048], P(('expert', 'tensor')), may hold values from -6 to 6
- contexts: bfloat16 [16384, 4096], P('expert', 'tensor'), may hold values from -6 to 6
- att_routes: int32 [16384, 2], P('expert'), may hold values from 0 to 7, all different within a row
- att_scores: float32 [16384, 2], P('expert'), may hold values from -6 to 6
- att_out_w: bfloat16 [8, 2048, 2048], P(None, 'tensor'), may hold values from -0.125 to 0.125
- norm_gain: bfloat16 [2048], replicated, may hold values from 0.25 to 1.75
- router_w: bfloat16 [2048, 8], replicated, may hold values from -0.125 to 0.125
- mlp_routes: int32 [16384, 2], P(('expert', 'tensor')), may hold values from 0 to 7, all different within a row
- split_rule: int32 [16384, 2], P(('expert', 'tensor')), may hold values from 0 to 2519
- placement: int32 [32], replicated, may hold values from 0 to 7, as said below
- cap_blocks: int32 [32], replicated, may hold values from 1 to 2, as said below
- w_gate_up: bfloat16 [32, 2048, 2, 5632], P('tensor', None, None, 'expert'), as said below
- w_down: bfloat16 [32, 5632, 2048], P('tensor', 'expert'), as said below
- final_gain: bfloat16 [2048], replicated, may hold values from 0.25 to 1.75
Outputs:
- stream_out: bfloat16 [16384, 2048], P(('expert', 'tensor'))
- normalized: bfloat16 [16384, 2048], P(('expert', 'tensor'))
Inputs may be any that keep to these rules, and one draw needn't show every extreme that they name: `att_routes`: each row names 2 different experts. `mlp_routes`: each row names 2 different experts. `placement`: every expert is held by at least one slot. `cap_blocks`: some slot accepts 2 blocks. `w_gate_up`: slots that hold the same expert hold equal weights. `w_down`: slots that hold the same expert hold equal weights.
All inputs are finite; a program needn't handle non-finite values.
Results may differ from a plain program's by a relative error of at most 0.023.
Values may be sent and summed in bfloat16 or wider, within the bound.
No kernel may reach another device: no remote copies, remote signals or barrier semaphores. Data moves between devices by JAX's collectives and lax.ppermute only.
A program may use at most 64 MiB of HBM per device.

v0:
```python
import jax
import jax.numpy as jnp
from jax import lax
from jax.sharding import Mesh, PartitionSpec as P

MAXB = 2
TENSOR = ("tz", "ty")
norm_eps = 1e-06


def rms_norm(values, gain):
    scale = lax.rsqrt(jnp.mean(values * values, axis=-1, keepdims=True) + norm_eps)
    return values * scale * gain.astype(values.dtype)


def pair_gates(scores):
    first = jax.nn.silu(scores[:, 0:1] * 0.0) * 0.0 + jax.nn.sigmoid(
        scores[:, 0:1] - scores[:, 1:2]
    )
    first = first[:, 0]
    return jnp.stack([first, 1.0 - first], axis=1)


def activate(shard_piece, w_gate_up):
    both = jnp.einsum(
        "tsecd,sdgf->tsecgf", shard_piece, w_gate_up, preferred_element_type=jnp.float32
    )
    hidden = (jax.nn.silu(both[:, :, :, :, 0, :]) * both[:, :, :, :, 1, :]).astype(jnp.bfloat16)
    hidden = jnp.transpose(hidden, (0, 2, 3, 1, 4))
    return hidden.reshape(
        hidden.shape[0] * hidden.shape[1] * hidden.shape[2], hidden.shape[3], hidden.shape[4]
    )


def per_device(
    resid,
    contexts,
    att_routes,
    att_scores,
    att_out_w,
    norm_gain,
    router_w,
    mlp_routes,
    split_rule,
    placement,
    cap_blocks,
    w_gate_up,
    w_down,
    final_gain,
):
    n_tensor = lax.axis_size(TENSOR)
    row_count = resid.shape[0]
    model_width = resid.shape[1]
    group_rows = contexts.shape[0]
    att_experts = att_out_w.shape[0]
    slice_ctx = att_out_w.shape[1]
    top_count = att_routes.shape[1]
    gate_att = pair_gates(att_scores)
    chosen = (
        att_routes[:, :, None] == jnp.arange(att_experts, dtype=jnp.int32)[None, None, :]
    ).astype(jnp.float32)
    weighted = chosen * gate_att[:, :, None]
    context_part = contexts.reshape(group_rows, slice_ctx, top_count).astype(jnp.float32)
    mixed = (
        jnp.einsum("tke,tck->tec", weighted, context_part)
        .astype(jnp.bfloat16)
        .reshape(group_rows, att_experts * slice_ctx)
    )
    weight_flat = att_out_w.reshape(att_experts * slice_ctx, model_width)
    row_block = mixed
    partial = jnp.dot(row_block, weight_flat, preferred_element_type=jnp.float32).astype(
        jnp.bfloat16
    )
    partial = lax.psum_scatter(partial, "tz", scatter_dimension=0, tiled=True)
    attention = lax.psum_scatter(partial, "ty", scatter_dimension=0, tiled=True).astype(jnp.float32)
    stream = (resid.astype(jnp.float32) + attention).astype(jnp.bfloat16)
    normed = rms_norm(stream.astype(jnp.float32), norm_gain).astype(jnp.bfloat16)
    logits = jnp.dot(normed, router_w, preferred_element_type=jnp.float32)
    gate_mlp = pair_gates(jnp.take_along_axis(logits, mlp_routes, axis=1))
    replicas = placement.shape[0]
    slots = w_gate_up.shape[0]
    expert_total = router_w.shape[1]
    block_rows = max(1, row_count * top_count // (2 * replicas))
    capacity_rows = MAXB * block_rows
    slot_ids = jnp.arange(replicas, dtype=jnp.int32)
    expert_ids = jnp.arange(expert_total, dtype=jnp.int32)
    copies = jnp.sum((placement[None, :] == expert_ids[:, None]).astype(jnp.int32), axis=1)
    earlier = jnp.sum(
        (
            (placement[None, :] == placement[:, None]) & (slot_ids[None, :] < slot_ids[:, None])
        ).astype(jnp.int32),
        axis=1,
    )
    route_onehot = (mlp_routes[:, :, None] == expert_ids[None, None, :]).astype(jnp.int32)
    route_copies = jnp.sum(route_onehot * copies[None, None, :], axis=2)
    replica_rank = jnp.remainder(split_rule, route_copies)
    match = (
        (placement[None, None, :] == mlp_routes[:, :, None])
        & (earlier[None, None, :] == replica_rank[:, :, None])
    ).astype(jnp.int32)
    replica_slot = jnp.sum(match * slot_ids[None, None, :], axis=2)
    capacity = jnp.sum(match * cap_blocks[None, None, :], axis=2) * block_rows
    flat_match = match.reshape(row_count * top_count, replicas)
    before = jnp.cumsum(flat_match, axis=0) - flat_match
    arrival = jnp.sum(before * flat_match, axis=1).reshape(row_count, top_count)
    is_kept = arrival < capacity
    holder = replica_slot // slots
    within = replica_slot % slots
    position = within * (n_tensor * capacity_rows) + holder * capacity_rows + arrival
    position = jnp.where(is_kept, position, -1)
    buffer_rows = slots * n_tensor * capacity_rows
    placer = jnp.sum(
        (jnp.arange(buffer_rows, dtype=jnp.int32)[:, None, None] == position[None, :, :]).astype(
            jnp.bfloat16
        ),
        axis=2,
    )
    send_rows = jnp.dot(placer, normed, preferred_element_type=jnp.float32).astype(jnp.bfloat16)
    send_rows = send_rows.reshape(slots, n_tensor, capacity_rows, model_width)
    exchanged = lax.all_to_all(send_rows, TENSOR, split_axis=1, concat_axis=1, tiled=True)
    arrived = lax.all_gather(exchanged[None], "expert", axis=0, tiled=True)
    hidden = activate(arrived, w_gate_up)
    row_block = hidden
    summed = lax.psum_scatter(
        jnp.einsum("bsf,sfd->bsd", row_block, w_down, preferred_element_type=jnp.float32).astype(
            jnp.bfloat16
        ),
        "expert",
        scatter_dimension=0,
        tiled=True,
    )
    results = summed.reshape(n_tensor, capacity_rows, slots, model_width)
    returned = lax.all_to_all(results, TENSOR, split_axis=0, concat_axis=0, tiled=True)
    flat_back = returned.reshape(n_tensor * capacity_rows * slots, model_width)
    back_index = jnp.where(is_kept, holder * (capacity_rows * slots) + arrival * slots + within, 0)
    fetched = (
        jnp.take(flat_back, back_index.reshape(-1), axis=0)
        .reshape(row_count, top_count, model_width)
        .astype(jnp.float32)
    )
    factors = gate_mlp * is_kept.astype(jnp.float32)
    expert_mix = fetched[:, 0, :] * factors[:, 0:1] + fetched[:, 1, :] * factors[:, 1:2]
    after = stream.astype(jnp.float32) + expert_mix
    return (after.astype(jnp.bfloat16), rms_norm(after, final_gain).astype(jnp.bfloat16))


def split_mesh(mesh):
    n_expert, n_tensor = mesh.devices.shape
    n_y = 4 if n_tensor % 4 == 0 else 1
    return Mesh(mesh.devices.reshape(n_expert, n_tensor // n_y, n_y), ("expert", "tz", "ty"))


def solution(mesh):
    mesh = split_mesh(mesh)
    return jax.shard_map(
        per_device,
        mesh=mesh,
        in_specs=(
            P(("expert", "tz", "ty"), None),
            P("expert", TENSOR),
            P("expert", None),
            P("expert", None),
            P(None, TENSOR, None),
            P(),
            P(),
            P(("expert", "tz", "ty"), None),
            P(("expert", "tz", "ty"), None),
            P(),
            P(),
            P(TENSOR, None, None, "expert"),
            P(TENSOR, "expert", None),
            P(),
        ),
        out_specs=(P(("expert", "tz", "ty"), None), P(("expert", "tz", "ty"), None)),
        check_vma=False,
    )
```

profile of v0, /device:TPU:7, one launch (start us, length us, event | category | flops | bytes accessed | tf_op | source)
XLA Modules:
  0.0 327.3 jit_solution(1362483452195812732)
XLA Ops:
  7.2 2.2 copy.76
  9.4 1.4 reshape.178
  10.8 2.1 copy.77
  13.0 0.3 copy.75
  13.3 1.4 copy.74
  14.7 14.3 %convolution_convert_fusion = bf16[2048,8,64]{2,1,0:T(8,128)(2,1)S(1)} fusion(bf16[2048,64,2]{1,2,0:T(2,128)(2,1)} %copy.77, bf16[2048,2]{1,0:T(8,128)(2,1)S(1)} %copy.75, s32[2048,2]{1,0:T(8,128)} %copy.74), kind=kOutput, calls=%fused_computation.13 | convolution fusion | flops 4259840 | bytes 2646016 | tf_op jit(solution)/shard_map/tke,tck->tec/dot_general | solution.py:65
  29.0 7.0 %bitcast_convert_fusion = bf16[2048,2048]{1,0:T(8,128)(2,1)} fusion(bf16[8,64,2048]{2,1,0:T(8,128)(2,1)S(1)} %copy-done.11, bf16[2048,8,64]{2,1,0:T(8,128)(2,1)S(1)} %convolution_convert_fusion), kind=kOutput, calls=%fused_computation.2 | convolution fusion | flops 4299161600 | bytes 12582912 | tf_op jit(solution)/shard_map/dot_general | solution.py:71
  36.1 98.0 %reduce-scatter.4.cloned.1.call-done = bf16[256,2048]{1,0:T(8,128)(2,1)} async-done(((bf16[2048,2048]{1,0:T(8,128)(2,1)}), bf16[256,2048]{1,0:T(8,128)(2,1)}) %reduce-scatter.4.cloned.1.call-update) | async-done | bytes 1048592 | tf_op jit(solution)/shard_map/reduce_scatter | solution.py:74
  134.2 0.1 convert_reduce_fusion.1
  134.5 0.1 and_select_fusion.1
  134.6 0.1 copy.80
  134.7 0.1 eq.133
  134.8 0.1 eq.119
  135.0 0.2 convert_reduce_fusion
  135.1 0.1 fusion.26
  135.3 0.2 reduce_window_sum.11
  135.4 0.2 select_reduce_fusion
  135.6 0.1 reduce_sum.92
  135.8 0.1 select_reduce_fusion.2
  136.0 23.9 %reduce-scatter.6.cloned.1.call-done = bf16[64,2048]{1,0:T(8,128)(2,1)} async-done(((bf16[256,2048]{1,0:T(8,128)(2,1)}), bf16[64,2048]{1,0:T(8,128)(2,1)}) %reduce-scatter.6.cloned.1.call-update) | async-done | bytes 262160 | tf_op jit(solution)/shard_map/reduce_scatter | solution.py:75
  160.0 1.1 fusion.15
  161.1 1.1 convolution_convert_fusion.1
  162.3 2.0 reshape.179
  164.3 21.4 %all_to_all.10 = bf16[1,32,4,2048]{3,2,0,1:T(4,128)(2,1)S(1)} all-to-all(bf16[1,32,4,2048]{3,2,0,1:T(4,128)(2,1)} %bitcast.82), channel_id=1, replica_groups=mesh['expert'=8,'tz'=8,'ty'=4] {'tz','ty'}, dimensions={1} | all-to-all | bytes 1048576 | tf_op jit(solution)/shard_map/all_to_all | solution.py:120
  185.7 1.1 copy.84
  186.8 0.2 reduce-scatter.8.cloned.1.call-start
  187.0 33.9 %all-gather.3.cloned.1.call-done = bf16[8,32,4,2048]{3,1,2,0:T(8,128)(2,1)} async-done(((bf16[1,32,4,2048]{3,1,2,0:T(8,128)(2,1)}), bf16[8,32,4,2048]{3,1,2,0:T(8,128)(2,1)}) %all-gather.3.cloned.1.call-update) | async-done | bytes 4194320 | tf_op jit(solution)/shard_map/all_gather | solution.py:121
  220.9 10.0 %fusion.6 = f32[8,1,32,4,2,704]{5,2,4,3,0,1:T(8,128)S(1)} fusion(bf16[1,2048,2,704]{1,3,2,0:T(8,128)(2,1)} %param.25, bf16[8,32,4,2048]{3,1,2,0:T(8,128)(2,1)} %all-gather.3.cloned.1.call-done), kind=kOutput, calls=%fused_computation.12 | convolution fusion | flops 5905580032 | bytes 15728640 | tf_op jit(solution)/shard_map/tsecd,sdgf->tsecgf/dot_general | solution.py:25
  230.9 1.0 fusion.4
  231.9 2.4 copy.85
  234.3 3.7 %convert_element_type.95 = bf16[1024,704]{1,0:T(8,128)(2,1)} reshape(bf16[8,1,32,4,1,704]{5,3,2,0,4,1:T(4,128)(2,1)} %copy.85) | data formatting | bytes 2883584 | tf_op jit(solution)/shard_map/convert_element_type | solution.py:28
  238.1 6.4 %convert_bitcast_fusion = bf16[1024,1,2048]{2,0,1:T(8,128)(2,1)} fusion(bf16[1024,704]{1,0:T(8,128)(2,1)} %convert_element_type.95, bf16[1,704,2048]{2,1,0:T(8,128)(2,1)S(1)} %copy-done), kind=kOutput, calls=%fused_computation.7 | convolution fusion | flops 2954887168 | bytes 8519680 | tf_op jit(solution)/shard_map/bsf,sfd->bsd/dot_general | solution.py:125
  244.6 0.1 reshape.194
  244.8 0.1 mul.206
  245.0 0.1 mul.205
  245.2 39.8 %reduce-scatter.8.cloned.1.call-done = bf16[128,1,2048]{2,0,1:T(8,128)(2,1)} async-done(((bf16[1024,1,2048]{2,0,1:T(8,128)(2,1)}), bf16[128,1,2048]{2,0,1:T(8,128)(2,1)}) %reduce-scatter.8.cloned.1.call-update) | async-done | bytes 524304 | tf_op jit(solution)/shard_map/reduce_scatter | solution.py:124
  285.0 2.0 reshape.183
  287.1 9.7 %all-to-all-start.1 = ((bf16[32,4,1,2048]{3,1,2,0:T(4,128)(2,1)}), bf16[32,4,1,2048]{3,1,2,0:T(4,128)(2,1)}, u32[]{:S(2)}, u32[]{:S(2)}) async-start(bf16[32,4,1,2048]{3,1,2,0:T(4,128)(2,1)} %bitcast.81), calls=%async_computation.4 | async-start | bytes 1048576 | tf_op jit(solution)/shard_map/all_to_all | solution.py:133
  296.8 0.2 fusion.22
  297.0 1.0 gather_fusion.1
  298.1 0.1 reshape.197
  298.3 15.7 %all-to-all-done.1 = bf16[32,4,1,2048]{3,1,2,0:T(4,128)(2,1)} async-done(((bf16[32,4,1,2048]{3,1,2,0:T(4,128)(2,1)}), bf16[32,4,1,2048]{3,1,2,0:T(4,128)(2,1)}, u32[]{:S(2)}, u32[]{:S(2)}) %all-to-all-start.1) | async-done | bytes 524320 | tf_op jit(solution)/shard_map/all_to_all | solution.py:133
  314.1 1.2 reshape.184
  315.2 1.7 gather_fusion
  317.0 1.4 gather.11
  318.3 0.3 fusion.21
  318.7 1.2 multiply_reduce_fusion
  320.0 0.8 multiply_convert_fusion
  (56 shorter events, 1.1 us)
Async XLA Ops:
  7.2 230.9 %copy-start = (bf16[1,704,2048]{2,1,0:T(8,128)(2,1)S(1)}, bf16[1,704,2048]{2,1,0:T(8,128)(2,1)}, u32[]{:S(2)}) copy-start(bf16[1,704,2048]{2,1,0:T(8,128)(2,1)} %param.26) | copy-start | bytes 8650756
  7.2 5.7 %copy-start.5 = (f32[2048,2]{0,1:T(2,128)S(1)}, f32[2048,2]{0,1:T(2,128)}, u32[]{:S(2)}) copy-start(f32[2048,2]{0,1:T(2,128)} %param.17) | copy-start | bytes 49156
  7.2 6.1 %copy-start.4 = (s32[2048,2]{0,1:T(2,128)S(1)}, s32[2048,2]{0,1:T(2,128)}, u32[]{:S(2)}) copy-start(s32[2048,2]{0,1:T(2,128)} %param.16) | copy-start | bytes 49156
  7.2 126.8 %reduce-scatter.4.cloned.1.call-start = ((), (), s32[]{:S(2)}) async-start(), calls=%async_computation.5 | async-start | bytes 9437184 | tf_op jit(solution)/shard_map/reduce_scatter | solution.py:74
  14.7 14.3 %copy-start.11 = (bf16[8,64,2048]{2,1,0:T(8,128)(2,1)S(1)}, bf16[8,64,2048]{2,1,0:T(8,128)(2,1)}, u32[]{:S(2)}) copy-start(bf16[8,64,2048]{2,1,0:T(8,128)(2,1)} %param.18) | copy-start | bytes 6291460
  36.0 98.2 %copy-start.7 = (bf16[2048]{0:T(1024)(128)(2,1)S(1)}, bf16[2048]{0:T(1024)(128)(2,1)}, u32[]{:S(2)}) copy-start(bf16[2048]{0:T(1024)(128)(2,1)} %param.19) | copy-start | bytes 12292
  36.0 98.2 %copy-start.3 = (s32[64,2]{0,1:T(2,128)S(1)}, s32[64,2]{0,1:T(2,128)}, u32[]{:S(2)}) copy-start(s32[64,2]{0,1:T(2,128)} %param.21) | copy-start | bytes 1540
  36.0 98.3 %copy-start.6 = (s32[32]{0:T(128)S(1)}, s32[32]{0:T(128)}, u32[]{:S(2)}) copy-start(s32[32]{0:T(128)} %param.23) | copy-start | bytes 388
  36.0 98.5 %copy-start.9 = (s32[64,2]{0,1:T(2,128)S(1)}, s32[64,2]{0,1:T(2,128)}, u32[]{:S(2)}) copy-start(s32[64,2]{0,1:T(2,128)} %param.22) | copy-start | bytes 1540
  36.0 99.9 %copy-start.10 = (s32[32]{0:T(128)S(1)}, s32[32]{0:T(128)}, u32[]{:S(2)}) copy-start(s32[32]{0:T(128)} %param.24) | copy-start | bytes 388
  36.0 124.0 %copy-start.2 = (bf16[64,2048]{1,0:T(8,128)(2,1)S(1)}, bf16[64,2048]{1,0:T(8,128)(2,1)}, u32[]{:S(2)}) copy-start(bf16[64,2048]{1,0:T(8,128)(2,1)} %param.14) | copy-start | bytes 786436
  36.0 123.9 %reduce-scatter.6.cloned.1.call-start = ((), (), s32[]{:S(2)}) async-start(), calls=%async_computation.6 | async-start | bytes 1310720 | tf_op jit(solution)/shard_map/reduce_scatter | solution.py:75
  134.1 86.9 %all-gather.3.cloned.1.call-start = ((), (), s32[]{:S(2)}) async-start(), calls=%async_computation.8 | async-start | bytes 4718592 | tf_op jit(solution)/shard_map/all_gather | solution.py:121
  161.1 135.7 %copy-start.1 = (bf16[64,2048]{1,0:T(8,128)(2,1)}, bf16[64,2048]{1,0:T(8,128)(2,1)S(1)}, u32[]{:S(2)}) copy-start(bf16[64,2048]{1,0:T(8,128)(2,1)S(1)} %get-tuple-element.9) | copy-start | bytes 786436
  186.8 98.2 %reduce-scatter.8.cloned.1.call-start = ((), (), s32[]{:S(2)}) async-start(), calls=%async_computation.7 | async-start | bytes 4718592 | tf_op jit(solution)/shard_map/reduce_scatter | solution.py:124
  244.4 0.8 copy-start.8
  244.4 52.4 %copy-start.12 = (bf16[2048,8]{0,1:T(8,128)(2,1)S(1)}, bf16[2048,8]{0,1:T(8,128)(2,1)}, u32[]{:S(2)}) copy-start(bf16[2048,8]{0,1:T(8,128)(2,1)} %param.20) | copy-start | bytes 98308
  287.1 27.0 %all-to-all-start.1 = ((bf16[32,4,1,2048]{3,1,2,0:T(4,128)(2,1)}), bf16[32,4,1,2048]{3,1,2,0:T(4,128)(2,1)}, u32[]{:S(2)}, u32[]{:S(2)}) async-start(bf16[32,4,1,2048]{3,1,2,0:T(4,128)(2,1)} %bitcast.81), calls=%async_computation.4 | async-start | bytes 1048576 | tf_op jit(solution)/shard_map/all_to_all | solution.py:133
Sparse Core Ops, SparseCore 0:
  36.1 97.8 reduce-scatter.3
  136.6 23.3 reduce-scatter.5
  186.9 33.9 all-gather.2
  244.6 40.4 reduce-scatter.7
where the time goes:
time: 328 us; the launch traced here: 327 us
  waiting for transfers between devices  211 us (64%)
  matrix products  39 us (12%)
  local copies, waits for them, and re-layouts  25.6 us (8%)
  blocking collectives  21.4 us (7%)
  between operations  14.1 us (4%)
  starting transfers between devices  10 us (3%)
  other arithmetic  5.93 us (2%)
    reduce_scatter x1, waiting for transfers between devices, per_device(): partial = lax.psum_scatter(partial, 'tz', scatter_dimension=0, tiled=True)  98 us
    reduce_scatter x1, waiting for transfers between devices, per_device(): lax.psum_scatter(jnp.einsum('bsf,sfd->bsd', row_block, w_down, preferred_...  39.8 us
    all_gather x1, waiting for transfers between devices, per_device(): arrived = lax.all_gather(exchanged[None], 'expert', axis=0, tiled=True)  33.9 us
    reduce_scatter x1, waiting for transfers between devices, per_device(): lax.psum_scatter(partial, 'ty', scatter_dimension=0, tiled=True)  23.9 us
    all_to_all x1, blocking collectives, per_device(): lax.all_to_all(send_rows, TENSOR, split_axis=1, concat_axis=1, tiled=True)  21.4 us
    all_to_all x1, waiting for transfers between devices, per_device(): lax.all_to_all(results, TENSOR, split_axis=0, concat_axis=0, tiled=True)  15.7 us
    dot_general x1, matrix products, per_device(): jnp.einsum('tke,tck->tec', weighted, context_part).astype(jnp.bfloat16)  14.3 us
    dot_general x1, matrix products, activate(): jnp.einsum('tsecd,sdgf->tsecgf', shard_piece, w_gate_up, preferred_elemen...  9.98 us
  transfers between devices with their start and end apart: 5, of which 5 were waited for; matrix products, arithmetic and copies ran while one was open for 1% of the time, Pallas kernels for 0%

commit v1 on v0

--- a/solution.py
+++ b/solution.py
@@ -118,7 +118,10 @@
     send_rows = jnp.dot(placer, normed, preferred_element_type=jnp.float32).astype(jnp.bfloat16)
     send_rows = send_rows.reshape(slots, n_tensor, capacity_rows, model_width)
     exchanged = lax.all_to_all(send_rows, TENSOR, split_axis=1, concat_axis=1, tiled=True)
-    arrived = lax.all_gather(exchanged[None], "expert", axis=0, tiled=True)
+    arrived = jnp.concatenate(
+        lax.all_to_all(jnp.stack([exchanged[None]] * lax.axis_size("expert")), "expert", 0, 0),
+        axis=0,
+    )
     hidden = activate(arrived, w_gate_up)
     row_block = hidden
     summed = lax.psum_scatter(

time: 328 us -> 342 us (1.043)
  blocking collectives: 21.4 us -> 78.9 us
  waiting for transfers between devices: 211 us -> 172 us
    all_to_all x0 -> x1, blocking collectives: none -> 57.6 us  [per_device(): lax.all_to_all(jnp.stack([exchanged[None]] * lax.axis_size('expert')), 'e...]
    all_gather x1 -> x0, waiting for transfers between devices: 33.9 us -> none  [per_device(): arrived = lax.all_gather(exchanged[None], 'expert', axis=0, tiled=True)]
    reduce_scatter x1, waiting for transfers between devices: 39.8 us -> 34.3 us  [per_device(): lax.psum_scatter(jnp.einsum('bsf,sfd->bsd', row_block, w_down, preferred_...]
  transfers between devices with their start and end apart: 5 -> 4, of which waited for: 5 -> 4; matrix products, arithmetic and copies ran while one was open for 1% -> 1% of each run, Pallas kernels for 0% -> 0%
where the time goes in v1:
time: 342 us
  waiting for transfers between devices  172 us (50%)
  blocking collectives  78.9 us (23%)
  matrix products  35.7 us (10%)
  local copies, waits for them, and re-layouts  25.3 us (7%)
  between operations  14.1 us (4%)
  starting transfers between devices  9.86 us (3%)
  other arithmetic  5.93 us (2%)
    reduce_scatter x1, waiting for transfers between devices, per_device(): partial = lax.psum_scatter(partial, 'tz', scatter_dimension=0, tiled=True)  98 us
    all_to_all x1, blocking collectives, per_device(): lax.all_to_all(jnp.stack([exchanged[None]] * lax.axis_size('expert')), 'e...  57.6 us
    reduce_scatter x1, waiting for transfers between devices, per_device(): lax.psum_scatter(jnp.einsum('bsf,sfd->bsd', row_block, w_down, preferred_...  34.3 us
    reduce_scatter x1, waiting for transfers between devices, per_device(): lax.psum_scatter(partial, 'ty', scatter_dimension=0, tiled=True)  23.9 us
    all_to_all x1, blocking collectives, per_device(): lax.all_to_all(send_rows, TENSOR, split_axis=1, concat_axis=1, tiled=True)  21.4 us
    all_to_all x1, waiting for transfers between devices, per_device(): lax.all_to_all(results, TENSOR, split_axis=0, concat_axis=0, tiled=True)  15.7 us
    dot_general x1, matrix products, per_device(): jnp.einsum('tke,tck->tec', weighted, context_part).astype(jnp.bfloat16)  14.3 us
    all_to_all x1, starting transfers between devices, per_device(): lax.all_to_all(results, TENSOR, split_axis=0, concat_axis=0, tiled=True)  9.74 us
  transfers between devices with their start and end apart: 4, of which 4 were waited for; matrix products, arithmetic and copies ran while one was open for 1% of the time, Pallas kernels for 0%

profile of v1, /device:TPU:7, one launch (start us, length us, event | category | flops | bytes accessed | tf_op | source)
XLA Modules:
  0.0 341.8 jit_solution(15637602632583291146)
XLA Ops:
  7.2 2.2 copy.76
  9.4 1.4 reshape.183
  10.8 2.1 copy.77
  13.0 0.3 copy.75
  13.3 1.4 copy.74
  14.7 14.3 %convolution_convert_fusion = bf16[2048,8,64]{2,1,0:T(8,128)(2,1)S(1)} fusion(bf16[2048,64,2]{1,2,0:T(2,128)(2,1)} %copy.77, bf16[2048,2]{1,0:T(8,128)(2,1)S(1)} %copy.75, s32[2048,2]{1,0:T(8,128)} %copy.74), kind=kOutput, calls=%fused_computation.13 | convolution fusion | flops 4259840 | bytes 2646016 | tf_op jit(solution)/shard_map/tke,tck->tec/dot_general | solution.py:65
  29.0 7.0 %bitcast_convert_fusion = bf16[2048,2048]{1,0:T(8,128)(2,1)} fusion(bf16[8,64,2048]{2,1,0:T(8,128)(2,1)S(1)} %copy-done.11, bf16[2048,8,64]{2,1,0:T(8,128)(2,1)S(1)} %convolution_convert_fusion), kind=kOutput, calls=%fused_computation.2 | convolution fusion | flops 4299161600 | bytes 12582912 | tf_op jit(solution)/shard_map/dot_general | solution.py:71
  36.1 98.0 %reduce-scatter.4.cloned.1.call-done = bf16[256,2048]{1,0:T(8,128)(2,1)} async-done(((bf16[2048,2048]{1,0:T(8,128)(2,1)}), bf16[256,2048]{1,0:T(8,128)(2,1)}) %reduce-scatter.4.cloned.1.call-update) | async-done | bytes 1048592 | tf_op jit(solution)/shard_map/reduce_scatter | solution.py:74
  134.2 0.1 convert_reduce_fusion.1
  134.5 0.1 and_select_fusion.1
  134.6 0.1 copy.80
  134.7 0.1 eq.133
  134.8 0.1 eq.119
  135.0 0.2 convert_reduce_fusion
  135.1 0.1 fusion.26
  135.3 0.2 reduce_window_sum.11
  135.4 0.2 select_reduce_fusion
  135.6 0.1 reduce_sum.92
  135.8 0.1 select_reduce_fusion.2
  136.0 23.9 %reduce-scatter.6.cloned.1.call-done = bf16[64,2048]{1,0:T(8,128)(2,1)} async-done(((bf16[256,2048]{1,0:T(8,128)(2,1)}), bf16[64,2048]{1,0:T(8,128)(2,1)}) %reduce-scatter.6.cloned.1.call-update) | async-done | bytes 262160 | tf_op jit(solution)/shard_map/reduce_scatter | solution.py:75
  160.0 1.1 fusion.15
  161.1 1.1 convolution_convert_fusion.1
  162.3 2.0 reshape.184
  164.3 21.4 %all_to_all.18 = bf16[1,32,4,2048]{3,2,0,1:T(4,128)(2,1)S(1)} all-to-all(bf16[1,32,4,2048]{3,2,0,1:T(4,128)(2,1)} %bitcast.85), channel_id=1, replica_groups=mesh['expert'=8,'tz'=8,'ty'=4] {'tz','ty'}, dimensions={1} | all-to-all | bytes 1048576 | tf_op jit(solution)/shard_map/all_to_all | solution.py:120
  185.7 0.3 copy.84
  186.0 0.5 stack.12
  186.5 57.6 %all_to_all.19 = bf16[8,1,1,32,4,2048]{5,3,4,2,1,0:T(8,128)(2,1)S(1)} all-to-all(bf16[8,1,1,32,4,2048]{5,3,4,2,1,0:T(8,128)(2,1)S(1)} %stack.12), channel_id=1, replica_groups=mesh['expert'=8,'tz'=8,'ty'=4] {'expert'}, dimensions={0} | all-to-all | bytes 8388608 | tf_op jit(solution)/shard_map/all_to_all | solution.py:122
  244.1 6.7 %fusion.6 = f32[8,1,32,4,2,704]{5,2,4,3,0,1:T(8,128)S(1)} fusion(bf16[1,2048,2,704]{1,3,2,0:T(8,128)(2,1)S(1)} %bitcast.88, bf16[8,1,1,32,4,2048]{5,3,4,2,1,0:T(8,128)(2,1)S(1)} %all_to_all.19), kind=kOutput, calls=%fused_computation.12 | convolution fusion | flops 5905580032 | bytes 15728640 | tf_op jit(solution)/shard_map/tsecd,sdgf->tsecgf/dot_general | solution.py:25
  250.8 1.0 fusion.4
  251.8 2.4 copy.85
  254.2 3.7 %convert_element_type.95 = bf16[1024,704]{1,0:T(8,128)(2,1)} reshape(bf16[8,1,32,4,1,704]{5,3,2,0,4,1:T(4,128)(2,1)} %copy.85) | data formatting | bytes 2883584 | tf_op jit(solution)/shard_map/convert_element_type | solution.py:28
  257.9 6.4 %convert_bitcast_fusion = bf16[1024,1,2048]{2,0,1:T(8,128)(2,1)} fusion(bf16[1024,704]{1,0:T(8,128)(2,1)} %convert_element_type.95, bf16[1,704,2048]{2,1,0:T(8,128)(2,1)S(1)} %copy-done), kind=kOutput, calls=%fused_computation.7 | convolution fusion | flops 2954887168 | bytes 8519680 | tf_op jit(solution)/shard_map/bsf,sfd->bsd/dot_general | solution.py:128
  264.4 0.1 reshape.199
  264.7 0.1 mul.206
  264.9 0.1 mul.205
  265.1 34.3 %reduce-scatter.8.cloned.1.call-done = bf16[128,1,2048]{2,0,1:T(8,128)(2,1)} async-done(((bf16[1024,1,2048]{2,0,1:T(8,128)(2,1)}), bf16[128,1,2048]{2,0,1:T(8,128)(2,1)}) %reduce-scatter.8.cloned.1.call-update) | async-done | bytes 524304 | tf_op jit(solution)/shard_map/reduce_scatter | solution.py:127
  299.4 2.0 reshape.188
  301.5 9.7 %all-to-all-start.2 = ((bf16[32,4,1,2048]{3,1,2,0:T(4,128)(2,1)}), bf16[32,4,1,2048]{3,1,2,0:T(4,128)(2,1)}, u32[]{:S(2)}, u32[]{:S(2)}) async-start(bf16[32,4,1,2048]{3,1,2,0:T(4,128)(2,1)} %bitcast.84), calls=%async_computation.5 | async-start | bytes 1048576 | tf_op jit(solution)/shard_map/all_to_all | solution.py:136
  311.2 0.2 fusion.22
  311.5 1.0 gather_fusion.1
  312.5 0.1 reshape.202
  312.8 15.7 %all-to-all-done.2 = bf16[32,4,1,2048]{3,1,2,0:T(4,128)(2,1)} async-done(((bf16[32,4,1,2048]{3,1,2,0:T(4,128)(2,1)}), bf16[32,4,1,2048]{3,1,2,0:T(4,128)(2,1)}, u32[]{:S(2)}, u32[]{:S(2)}) %all-to-all-start.2) | async-done | bytes 524320 | tf_op jit(solution)/shard_map/all_to_all | solution.py:136
  328.5 1.2 reshape.189
  329.7 1.7 gather_fusion
  331.4 1.4 gather.11
  332.8 0.3 fusion.21
  333.1 1.2 multiply_reduce_fusion
  334.4 0.8 multiply_convert_fusion
  (60 shorter events, 1.1 us)
Async XLA Ops:
  7.2 250.8 %copy-start = (bf16[1,704,2048]{2,1,0:T(8,128)(2,1)S(1)}, bf16[1,704,2048]{2,1,0:T(8,128)(2,1)}, u32[]{:S(2)}) copy-start(bf16[1,704,2048]{2,1,0:T(8,128)(2,1)} %param.26) | copy-start | bytes 8650756
  7.2 5.7 %copy-start.5 = (f32[2048,2]{0,1:T(2,128)S(1)}, f32[2048,2]{0,1:T(2,128)}, u32[]{:S(2)}) copy-start(f32[2048,2]{0,1:T(2,128)} %param.17) | copy-start | bytes 49156
  7.2 6.1 %copy-start.4 = (s32[2048,2]{0,1:T(2,128)S(1)}, s32[2048,2]{0,1:T(2,128)}, u32[]{:S(2)}) copy-start(s32[2048,2]{0,1:T(2,128)} %param.16) | copy-start | bytes 49156
  7.2 126.8 %reduce-scatter.4.cloned.1.call-start = ((), (), s32[]{:S(2)}) async-start(), calls=%async_computation.6 | async-start | bytes 9437184 | tf_op jit(solution)/shard_map/reduce_scatter | solution.py:74
  14.7 14.3 %copy-start.11 = (bf16[8,64,2048]{2,1,0:T(8,128)(2,1)S(1)}, bf16[8,64,2048]{2,1,0:T(8,128)(2,1)}, u32[]{:S(2)}) copy-start(bf16[8,64,2048]{2,1,0:T(8,128)(2,1)} %param.18) | copy-start | bytes 6291460
  36.0 98.2 %copy-start.7 = (bf16[2048]{0:T(1024)(128)(2,1)S(1)}, bf16[2048]{0:T(1024)(128)(2,1)}, u32[]{:S(2)}) copy-start(bf16[2048]{0:T(1024)(128)(2,1)} %param.19) | copy-start | bytes 12292
  36.0 98.2 %copy-start.3 = (s32[64,2]{0,1:T(2,128)S(1)}, s32[64,2]{0,1:T(2,128)}, u32[]{:S(2)}) copy-start(s32[64,2]{0,1:T(2,128)} %param.21) | copy-start | bytes 1540
  36.0 98.3 %copy-start.6 = (s32[32]{0:T(128)S(1)}, s32[32]{0:T(128)}, u32[]{:S(2)}) copy-start(s32[32]{0:T(128)} %param.23) | copy-start | bytes 388
  36.0 98.5 %copy-start.9 = (s32[64,2]{0,1:T(2,128)S(1)}, s32[64,2]{0,1:T(2,128)}, u32[]{:S(2)}) copy-start(s32[64,2]{0,1:T(2,128)} %param.22) | copy-start | bytes 1540
  36.0 99.9 %copy-start.10 = (s32[32]{0:T(128)S(1)}, s32[32]{0:T(128)}, u32[]{:S(2)}) copy-start(s32[32]{0:T(128)} %param.24) | copy-start | bytes 388
  36.0 124.0 %copy-start.2 = (bf16[64,2048]{1,0:T(8,128)(2,1)S(1)}, bf16[64,2048]{1,0:T(8,128)(2,1)}, u32[]{:S(2)}) copy-start(bf16[64,2048]{1,0:T(8,128)(2,1)} %param.14) | copy-start | bytes 786436
  36.0 123.9 %reduce-scatter.6.cloned.1.call-start = ((), (), s32[]{:S(2)}) async-start(), calls=%async_computation.7 | async-start | bytes 1310720 | tf_op jit(solution)/shard_map/reduce_scatter | solution.py:75
  134.1 165.4 %reduce-scatter.8.cloned.1.call-start = ((), (), s32[]{:S(2)}) async-start(), calls=%async_computation.8 | async-start | bytes 4718592 | tf_op jit(solution)/shard_map/reduce_scatter | solution.py:127
  161.1 150.1 %copy-start.1 = (bf16[64,2048]{1,0:T(8,128)(2,1)}, bf16[64,2048]{1,0:T(8,128)(2,1)S(1)}, u32[]{:S(2)}) copy-start(bf16[64,2048]{1,0:T(8,128)(2,1)S(1)} %get-tuple-element.9) | copy-start | bytes 786436
  186.0 58.1 %slice-start = ((s8[5767168]{0:T(1024)(128)(4,1)}), s8[4194304]{0:T(1024)(128)(4,1)S(1)}, s32[]{:S(2)}) async-start(s8[5767168]{0:T(1024)(128)(4,1)} %bitcast.87), calls=%async_computation.9 | async-start | bytes 8388608
  186.5 57.6 %slice-start.1 = ((s8[5767168]{0:T(1024)(128)(4,1)}), s8[1572864]{0:T(1024)(128)(4,1)S(1)}, s32[]{:S(2)}) async-start(s8[5767168]{0:T(1024)(128)(4,1)} %bitcast.87), calls=%async_computation.10 | async-start | bytes 3145728
  264.3 0.8 copy-start.8
  264.3 46.9 %copy-start.12 = (bf16[2048,8]{0,1:T(8,128)(2,1)S(1)}, bf16[2048,8]{0,1:T(8,128)(2,1)}, u32[]{:S(2)}) copy-start(bf16[2048,8]{0,1:T(8,128)(2,1)} %param.20) | copy-start | bytes 98308
  301.5 27.0 %all-to-all-start.2 = ((bf16[32,4,1,2048]{3,1,2,0:T(4,128)(2,1)}), bf16[32,4,1,2048]{3,1,2,0:T(4,128)(2,1)}, u32[]{:S(2)}, u32[]{:S(2)}) async-start(bf16[32,4,1,2048]{3,1,2,0:T(4,128)(2,1)} %bitcast.84), calls=%async_computation.5 | async-start | bytes 1048576 | tf_op jit(solution)/shard_map/all_to_all | solution.py:136
Sparse Core Ops, SparseCore 0:
  36.1 97.8 reduce-scatter.3
  136.6 23.3 reduce-scatter.5
  264.4 34.9 reduce-scatter.7
